TPU v7x, 256 devices: a whole 4x4x8 slice. The times are simulated.
256 devices in a mesh: tm: 16 (over z, core), tile: 16 (over x, y).
Axes of the slice: x: 4, y: 4, z: 8, core: 2. Of those that a mesh axis runs over, the one named last changes fastest.
Arguments:
- obs_values: bfloat16 [16, 32768, 128], P('tm', 'tile'), may hold values from -6 to 6
- obs_weight: bfloat16 [16, 32768, 128], P('tm', 'tile'), may hold values from 0.19921875 to 2
- obs_count: int32 [16, 32768], P('tm', 'tile'), may hold values from 32 to 128
- dest_tile: int32 [16, 32768, 1], P('tm', 'tile'), may hold values from 0 to 15; in each aligned block of 2048 rows (0 to 2047, 2048 to 4095, ..., all dimensions but the last counted through in order) at most 256 rows name the same one
- jac_index: int32 [16, 32768], P('tm', 'tile'), may hold values from 0 to 255
- jacobian: bfloat16 [16, 4096, 128, 128], P('tm', 'tile'), may hold values from -0.5 to 0.5
- jac_state: int32 [16, 4096], P('tm', 'tile'), may hold values from 0 to 63
- corr_blocks: bfloat16 [16, 768, 128, 128], P('tm', 'tile'), may hold values from -0.625 to 0.625
- corr_row: int32 [16, 768], P('tm', 'tile'), may hold values from 0 to 63
- corr_col: int32 [16, 768], P('tm', 'tile'), may hold values from 0 to 63
- time_coupling: bfloat16 [16, 1024, 128], P('tm', 'tile'), may hold values from 0.19921875 to 0.59765625
Outputs:
- product: bfloat16 [16, 32768, 128], P('tm', 'tile')
Inputs may be any that keep to these rules, and one draw needn't show every extreme that they name: `dest_tile`: in the rows of one device, no tile is named by more than 256 observation blocks, a bound that some block reaches.
All inputs are finite; a program needn't handle non-finite values.
Results may differ from a plain program's by a relative error of at most 0.0075.
Values may be sent and summed in bfloat16 or wider, within the bound.
No kernel may reach another device: no remote copies, remote signals or barrier semaphores. Data moves between devices by JAX's collectives and lax.ppermute only.
A program may use at most 64 MiB of HBM per device.

v0:
```python
import jax
import jax.numpy as jnp
from jax import lax
from jax.sharding import PartitionSpec as P


def from_behind(x, axis, by):
    length = lax.axis_size(axis)
    pairs = [(i, i + by) for i in range(length) if 0 <= i + by < length]
    return lax.ppermute(x, axis, pairs)


def shards(
    obs_values,
    obs_weight,
    obs_count,
    dest_tile,
    jac_index,
    jacobian,
    jac_state,
    corr_blocks,
    corr_row,
    corr_col,
    time_coupling,
):
    obs_total = obs_values.shape[1]
    block_width = obs_values.shape[2]
    jac_total = jacobian.shape[1]
    state_total = time_coupling.shape[1]
    lane_index = lax.broadcasted_iota(jnp.int32, (obs_total, block_width), 1)
    keeping = (lane_index < obs_count[0][:, None]).astype(jnp.float32)
    weighted = (
        obs_values[0].astype(jnp.float32) * obs_weight[0].astype(jnp.float32) * keeping
    ).astype(jnp.bfloat16)
    target = dest_tile[0, :, 0]
    column = jac_index[0]
    bin_id = target * jac_total + column
    row_ids = lax.broadcasted_iota(jnp.int32, (jac_total * lax.axis_size("tile"), obs_total), 0)
    picker = (row_ids == bin_id[None, :]).astype(jnp.bfloat16)
    summed = lax.psum_scatter(
        jnp.dot(picker, weighted, preferred_element_type=jnp.float32),
        "tile",
        scatter_dimension=0,
        tiled=True,
    )
    merged = summed.astype(jnp.bfloat16)
    spread = jnp.einsum("kij,ki->kj", jacobian[0], merged, preferred_element_type=jnp.float32)
    state_ids = lax.broadcasted_iota(jnp.int32, (state_total, jac_total), 0)
    owners = state_ids == jac_state[0][None, :]
    state = jnp.dot(owners.astype(jnp.float32), spread, precision=lax.Precision.HIGHEST).astype(
        jnp.bfloat16
    )
    corr_total = corr_blocks.shape[1]
    read_ids = lax.broadcasted_iota(jnp.int32, (corr_total, state_total), 1)
    reader = (read_ids == corr_col[0][:, None]).astype(jnp.bfloat16)
    source = jnp.dot(reader, state, preferred_element_type=jnp.float32).astype(jnp.bfloat16)
    mixing = jnp.einsum("cij,cj->ci", corr_blocks[0], source, preferred_element_type=jnp.float32)
    write_ids = lax.broadcasted_iota(jnp.int32, (state_total, corr_total), 0)
    writer = (write_ids == corr_row[0][None, :]).astype(jnp.float32)
    spatial = jnp.dot(writer, mixing, precision=lax.Precision.HIGHEST).astype(jnp.bfloat16)
    coupling = time_coupling[0]
    earlier = from_behind(spatial, "tm", 1)
    later_state, later_coupling = from_behind((spatial, coupling), "tm", -1)
    coupled = (
        spatial.astype(jnp.float32)
        + coupling.astype(jnp.float32) * earlier.astype(jnp.float32)
        + later_coupling.astype(jnp.float32) * later_state.astype(jnp.float32)
    ).astype(jnp.bfloat16)
    local_state = jnp.dot(
        owners.T.astype(jnp.bfloat16), coupled, preferred_element_type=jnp.float32
    ).astype(jnp.bfloat16)
    model_obs = jnp.einsum(
        "kij,kj->ki", jacobian[0], local_state, preferred_element_type=jnp.float32
    ).astype(jnp.bfloat16)
    portion = lax.all_gather(model_obs, "tile", axis=0, tiled=True)
    columns = lax.broadcasted_iota(jnp.int32, (obs_total, portion.shape[0]), 1)
    picker = (bin_id[:, None] == columns).astype(jnp.bfloat16)
    gathered = jnp.dot(picker, portion, preferred_element_type=jnp.float32)
    return (gathered * keeping).astype(jnp.bfloat16)[None]


def solution(mesh):
    in_specs = (
        P("tm", "tile", None),
        P("tm", "tile", None),
        P("tm", "tile"),
        P("tm", "tile", None),
        P("tm", "tile"),
        P("tm", "tile", None, None),
        P("tm", "tile"),
        P("tm", "tile", None, None),
        P("tm", "tile"),
        P("tm", "tile"),
        P("tm", "tile", None),
    )
    out_specs = P("tm", "tile", None)
    return jax.shard_map(shards, mesh=mesh, in_specs=in_specs, out_specs=out_specs, check_vma=False)
```

profile of v0, /device:TPU:2, one launch (start us, length us, event | category | flops | bytes accessed | tf_op | source)
XLA Modules:
  0.0 185.7 jit_solution(13283383729035749452)
XLA Ops:
  6.5 0.0 copy-start
  6.5 0.0 reduce-scatter.2.cloned.1.call-start
  6.5 0.8 bitcast_add_fusion
  7.4 0.0 copy-start.3
  7.4 8.6 %fusion = f32[4096,128]{1,0:T(8,128)} fusion(s32[2048]{0:T(1024)S(1)} %bitcast.51, bf16[1,2048,128]{2,1,0:T(8,128)(2,1)} %param.12, bf16[1,2048,128]{2,1,0:T(8,128)(2,1)} %param.11, s32[2048]{0:T(1024)} %bitcast.55), kind=kOutput, calls=%fused_computation.2 | convolution fusion | flops 2157445120 | bytes 3162112 | tf_op jit(solution)/shard_map/dot_general | solution.py:41
  16.0 0.0 copy-start.4
  16.0 0.0 copy-start.7
  16.0 0.0 copy-start.5
  16.0 0.0 reduce-scatter.2.cloned.1.call-update
  16.0 0.0 all-gather.2.cloned.1.call-start
  16.1 0.0 copy-done.3
  16.1 1.3 collective-permute-start.1
  17.4 81.6 %reduce-scatter.2.cloned.1.call-done = f32[256,128]{1,0:T(8,128)} async-done(((f32[4096,128]{1,0:T(8,128)}), f32[256,128]{1,0:T(8,128)}) %reduce-scatter.2.cloned.1.call-update) | async-done | bytes 131088 | tf_op jit(solution)/shard_map/reduce_scatter | solution.py:40
  99.0 0.9 convert_bitcast_fusion
  99.9 0.0 copy-start.2
  99.9 0.0 copy-start.1
  99.9 0.0 copy-start.6
  99.9 5.7 %fusion.6 = f32[256,1,128]{2,1,0:T(1,128)S(1)} fusion(bf16[1,256,128,128]{3,2,1,0:T(8,128)(2,1)} %param.16, bf16[256,128,1]{1,0,2:T(8,128)(2,1)S(1)} %convert_bitcast_fusion), kind=kOutput, calls=%fused_computation.8 | convolution fusion | flops 8388608 | bytes 8585216 | tf_op jit(solution)/shard_map/kij,ki->kj/dot_general | solution.py:47
  105.6 0.0 copy-done.4
  105.6 0.2 convolution_convert_fusion.2
  105.8 0.0 copy-done.7
  105.8 0.2 fusion.14
  106.0 0.0 copy-done
  106.0 0.9 fusion.11
  106.9 0.0 copy-done.5
  106.9 0.2 convolution_convert_fusion.1
  107.1 1.3 collective-permute-start
  108.4 1.5 collective-permute-start.2
  109.9 0.0 collective-permute-done.1
  109.9 0.0 collective-permute-done
  109.9 3.4 %collective-permute-done.2 = bf16[64,128]{1,0:T(8,128)(2,1)S(1)} collective-permute-done((bf16[64,128]{1,0:T(8,128)(2,1)S(1)}, bf16[64,128]{1,0:T(8,128)(2,1)S(1)}, u32[]{:S(2)}, u32[]{:S(2)}) %collective-permute-start.2) | collective-permute-done | bytes 16416 | tf_op jit(solution)/shard_map/ppermute | solution.py:10
  113.3 0.2 fusion.13
  113.5 7.8 %fusion.4 = f32[256,1,128]{2,1,0:T(1,128)S(1)} fusion(bf16[1,256,128,128]{3,2,1,0:T(8,128)(2,1)} %param.16, bf16[256,128,1]{1,0,2:T(8,128)(2,1)S(1)} %fusion.13), kind=kOutput, calls=%fused_computation.6 | convolution fusion | flops 8388608 | bytes 8585216 | tf_op jit(solution)/shard_map/kij,kj->ki/dot_general | solution.py:72
  121.3 0.7 convert_element_type.71
  121.9 0.0 all-gather.2.cloned.1.call-update
  121.9 0.0 copy-done.2
  122.0 0.0 copy-done.1
  122.0 49.3 %all-gather.2.cloned.1.call-done = bf16[4096,128]{1,0:T(8,128)(2,1)} async-done(((bf16[256,128]{1,0:T(8,128)(2,1)}), bf16[4096,128]{1,0:T(8,128)(2,1)}) %all-gather.2.cloned.1.call-update) | async-done | bytes 1048592 | tf_op jit(solution)/shard_map/all_gather | solution.py:75
  171.3 0.0 copy-done.6
  171.3 7.6 %fusion.10 = bf16[1,2048,128]{2,1,0:T(8,128)(2,1)} fusion(bf16[4096,128]{1,0:T(8,128)(2,1)} %all-gather.2.cloned.1.call-done, s32[2048]{0:T(1024)S(1)} %add.18, s32[2048]{0:T(1024)S(1)} %bitcast.56), kind=kOutput, calls=%fused_computation.12 | convolution fusion | flops 2156658688 | bytes 1589248 | tf_op jit(solution)/shard_map/dot_general | solution.py:78
  (2 shorter events, 0.0 us)
Async XLA Ops:
  6.5 99.5 %copy-start = (bf16[1,48,128,128]{3,2,1,0:T(8,128)(2,1)S(1)}, bf16[1,48,128,128]{3,2,1,0:T(8,128)(2,1)}, u32[]{:S(2)}) copy-start(bf16[1,48,128,128]{3,2,1,0:T(8,128)(2,1)} %param.18) | copy-start | bytes 4718596
  6.5 92.5 %reduce-scatter.2.cloned.1.call-start = ((), (), s32[]{:S(2)}) async-start(), calls=%async_computation.1 | async-start | bytes 2228224 | tf_op jit(solution)/shard_map/reduce_scatter | solution.py:40
  7.4 8.7 %copy-start.3 = (bf16[1,64,128]{2,1,0:T(8,128)(2,1)S(1)}, bf16[1,64,128]{2,1,0:T(8,128)(2,1)}, u32[]{:S(2)}) copy-start(bf16[1,64,128]{2,1,0:T(8,128)(2,1)} %param.21) | copy-start | bytes 49156
  16.0 89.6 %copy-start.4 = (s32[1,256]{1,0:T(1,128)S(1)}, s32[1,256]{1,0:T(1,128)}, u32[]{:S(2)}) copy-start(s32[1,256]{1,0:T(1,128)} %param.17) | copy-start | bytes 3076
  16.0 89.8 %copy-start.7 = (s32[1,48]{1,0:T(1,128)S(1)}, s32[1,48]{1,0:T(1,128)}, u32[]{:S(2)}) copy-start(s32[1,48]{1,0:T(1,128)} %param.20) | copy-start | bytes 580
  16.0 90.9 %copy-start.5 = (s32[1,48]{1,0:T(1,128)S(1)}, s32[1,48]{1,0:T(1,128)}, u32[]{:S(2)}) copy-start(s32[1,48]{1,0:T(1,128)} %param.19) | copy-start | bytes 580
  16.0 155.3 %all-gather.2.cloned.1.call-start = ((), (), s32[]{:S(2)}) async-start(), calls=%async_computation.2 | async-start | bytes 1114112 | tf_op jit(solution)/shard_map/all_gather | solution.py:75
  16.1 93.8 %collective-permute-start.1 = (bf16[64,128]{1,0:T(8,128)(2,1)S(1)}, bf16[64,128]{1,0:T(8,128)(2,1)S(1)}, u32[]{:S(2)}, u32[]{:S(2)}) collective-permute-start(bf16[64,128]{1,0:T(8,128)(2,1)S(1)} %bitcast.50), channel_id=1, source_target_pairs={{16,0},{32,16},{48,32},{64,48},{80,64},{96,80},{112,96},{128,112},... | collective-permute-start | bytes 49160 | tf_op jit(solution)/shard_map/ppermute | solution.py:10
  99.9 22.0 %copy-start.2 = (s32[1,2048,1]{1,2,0:T(1,128)S(1)}, s32[1,2048,1]{1,2,0:T(1,128)}, u32[]{:S(2)}) copy-start(s32[1,2048,1]{1,2,0:T(1,128)} %param.14) | copy-start | bytes 24580
  99.9 22.1 %copy-start.1 = (s32[1,2048]{1,0:T(1,128)S(1)}, s32[1,2048]{1,0:T(1,128)}, u32[]{:S(2)}) copy-start(s32[1,2048]{1,0:T(1,128)} %param.15) | copy-start | bytes 24580
  99.9 71.4 %copy-start.6 = (s32[1,2048]{1,0:T(1,128)S(1)}, s32[1,2048]{1,0:T(1,128)}, u32[]{:S(2)}) copy-start(s32[1,2048]{1,0:T(1,128)} %param.13) | copy-start | bytes 24580
  107.1 2.8 %collective-permute-start = (bf16[64,128]{1,0:T(8,128)(2,1)S(1)}, bf16[64,128]{1,0:T(8,128)(2,1)S(1)}, u32[]{:S(2)}, u32[]{:S(2)}) collective-permute-start(bf16[64,128]{1,0:T(8,128)(2,1)S(1)} %convolution_convert_fusion.1), channel_id=1, source_target_pairs={{0,16},{16,32},{32,48},{48,64},{64,80},{80,96},{96,112},{112,128},... | collective-permute-start | bytes 49160 | tf_op jit(solution)/shard_map/ppermute | solution.py:10
  108.4 4.9 %collective-permute-start.2 = (bf16[64,128]{1,0:T(8,128)(2,1)S(1)}, bf16[64,128]{1,0:T(8,128)(2,1)S(1)}, u32[]{:S(2)}, u32[]{:S(2)}) collective-permute-start(bf16[64,128]{1,0:T(8,128)(2,1)S(1)} %convolution_convert_fusion.1), channel_id=1, source_target_pairs={{16,0},{32,16},{48,32},{64,48},{80,64},{96,80},{112,96},{128,112},... | collective-permute-start | bytes 49160 | tf_op jit(solution)/shard_map/ppermute | solution.py:10
Sparse Core Ops, SparseCore 0:
  16.1 82.8 reduce-scatter.1
  122.1 49.1 all-gather.1
where the time goes:
time: 186 us
  waiting for transfers between devices  134 us (72%)
  matrix products  31.3 us (17%)
  between operations  13.5 us (7%)
  starting transfers between devices  4.1 us (2%)
  other arithmetic  2.44 us (1%)
    reduce_scatter x1, waiting for transfers between devices, shards(): lax.psum_scatter(jnp.dot(picker, weighted, preferred_element_type=jnp.flo...  81.6 us
    all_gather x1, waiting for transfers between devices, shards(): portion = lax.all_gather(model_obs, 'tile', axis=0, tiled=True)  49.3 us
    dot_general x1, matrix products, shards(): jnp.dot(picker, weighted, preferred_element_type=jnp.float32)  8.59 us
    dot_general x1, matrix products, shards(): jnp.einsum('kij,kj->ki', jacobian[0], local_state, preferred_element_type...  7.78 us
    dot_general x1, matrix products, shards(): gathered = jnp.dot(picker, portion, preferred_element_type=jnp.float32)  7.57 us
    dot_general x1, matrix products, shards(): jnp.einsum('kij,ki->kj', jacobian[0], merged, preferred_element_type=jnp....  5.66 us
    ppermute x3, starting transfers between devices, from_behind(): return lax.ppermute(x, axis, pairs)  4.06 us
  transfers between devices with their start and end apart: 5, of which 3 were waited for; matrix products, arithmetic and copies ran while one was open for 4% of the time, Pallas kernels for 0%

commit v1 on v0

--- a/solution.py
+++ b/solution.py
@@ -2,6 +2,27 @@
 import jax.numpy as jnp
 from jax import lax
 from jax.sharding import PartitionSpec as P
+
+
+def gather_around(value, axis, dim):
+    devices, position, width = (lax.axis_size(axis), lax.axis_index(axis), value.shape[dim])
+    upward = [(i, (i + 1) % devices) for i in range(devices)]
+    left = [(i, (i - 1) % devices) for i in range(devices)]
+    filled = jnp.zeros((*value.shape[:dim], devices * width, *value.shape[dim + 1 :]), value.dtype)
+    filled = lax.dynamic_update_slice_in_dim(filled, value, position * width, axis=dim)
+    from_left = from_right = value
+    middle = devices // 2
+    for step in range(1, middle + 1):
+        from_left = lax.ppermute(from_left, axis, upward)
+        filled = lax.dynamic_update_slice_in_dim(
+            filled, from_left, (position - step) % devices * width, axis=dim
+        )
+        if step < devices - middle:
+            from_right = lax.ppermute(from_right, axis, left)
+            filled = lax.dynamic_update_slice_in_dim(
+                filled, from_right, (position + step) % devices * width, axis=dim
+            )
+    return filled
 
 
 def from_behind(x, axis, by):
@@ -72,7 +93,7 @@
     model_obs = jnp.einsum(
         "kij,kj->ki", jacobian[0], local_state, preferred_element_type=jnp.float32
     ).astype(jnp.bfloat16)
-    portion = lax.all_gather(model_obs, "tile", axis=0, tiled=True)
+    portion = gather_around(model_obs, "tile", 0)
     columns = lax.broadcasted_iota(jnp.int32, (obs_total, portion.shape[0]), 1)
     picker = (bin_id[:, None] == columns).astype(jnp.bfloat16)
     gathered = jnp.dot(picker, portion, preferred_element_type=jnp.float32)

time: 186 us -> 198 us (1.065)
  the two profiles are of different devices: /device:TPU:2 before, /device:TPU:32 now
where the time goes in v1:
time: 198 us; the launch traced here: 197 us
  waiting for transfers between devices  105 us (53%)
  starting transfers between devices  45.6 us (23%)
  matrix products  30.7 us (16%)
  between operations  13.9 us (7%)
    reduce_scatter x1, waiting for transfers between devices, shards(): lax.psum_scatter(jnp.dot(picker, weighted, preferred_element_type=jnp.flo...  80.8 us
    ppermute x7, starting transfers between devices, gather_around(): from_right = lax.ppermute(from_right, axis, left)  36.7 us
    ppermute x8, waiting for transfers between devices, gather_around(): from_left = lax.ppermute(from_left, axis, upward)  22.6 us
    dot_general x1, matrix products, shards(): jnp.dot(picker, weighted, preferred_element_type=jnp.float32)  8.57 us
    dot_general x1, matrix products, shards(): jnp.einsum('kij,kj->ki', jacobian[0], local_state, preferred_element_type...  7.78 us
    ppermute x3, starting transfers between devices, from_behind(): return lax.ppermute(x, axis, pairs)  7.61 us
    dot_general x1, matrix products, shards(): gathered = jnp.dot(picker, portion, preferred_element_type=jnp.float32)  7.01 us
    dot_general x1, matrix products, shards(): jnp.einsum('kij,ki->kj', jacobian[0], merged, preferred_element_type=jnp....  5.65 us
  transfers between devices with their start and end apart: 19, of which 10 were waited for; matrix products, arithmetic and copies ran while one was open for 4% of the time, Pallas kernels for 0%

profile of v1, /device:TPU:32, one launch (start us, length us, event | category | flops | bytes accessed | tf_op | source)
XLA Modules:
  0.0 197.3 jit_solution(16818959264797003915)
XLA Ops:
  6.5 0.0 copy-start
  6.5 0.0 reduce-scatter.2.cloned.1.call-start
  6.5 0.8 bitcast_add_fusion
  7.4 0.0 copy-start.3
  7.4 8.6 %fusion = f32[4096,128]{1,0:T(8,128)} fusion(s32[2048]{0:T(1024)S(1)} %bitcast.51, bf16[1,2048,128]{2,1,0:T(8,128)(2,1)} %param.12, bf16[1,2048,128]{2,1,0:T(8,128)(2,1)} %param.11, s32[2048]{0:T(1024)} %bitcast.55), kind=kOutput, calls=%fused_computation.2 | convolution fusion | flops 2157445120 | bytes 3162112 | tf_op jit(solution)/shard_map/dot_general | solution.py:62
  16.0 0.0 copy-start.4
  16.0 0.0 copy-start.7
  16.0 0.0 copy-start.5
  16.0 0.0 reduce-scatter.2.cloned.1.call-update
  16.0 0.0 copy-done.3
  16.0 2.1 %collective-permute-start.1 = (bf16[64,128]{1,0:T(8,128)(2,1)S(1)}, bf16[64,128]{1,0:T(8,128)(2,1)S(1)}, u32[]{:S(2)}, u32[]{:S(2)}) collective-permute-start(bf16[64,128]{1,0:T(8,128)(2,1)S(1)} %bitcast.50), channel_id=1, source_target_pairs={{16,0},{32,16},{48,32},{64,48},{80,64},{96,80},{112,96},{128,112},... | collective-permute-start | bytes 49160 | tf_op jit(solution)/shard_map/ppermute | solution.py:31
  18.1 80.8 %reduce-scatter.2.cloned.1.call-done = f32[256,128]{1,0:T(8,128)} async-done(((f32[4096,128]{1,0:T(8,128)}), f32[256,128]{1,0:T(8,128)}) %reduce-scatter.2.cloned.1.call-update) | async-done | bytes 131088 | tf_op jit(solution)/shard_map/reduce_scatter | solution.py:61
  98.9 0.9 convert_bitcast_fusion
  99.8 5.7 %fusion.6 = f32[256,1,128]{2,1,0:T(1,128)S(1)} fusion(bf16[1,256,128,128]{3,2,1,0:T(8,128)(2,1)} %param.16, bf16[256,128,1]{1,0,2:T(8,128)(2,1)S(1)} %convert_bitcast_fusion), kind=kOutput, calls=%fused_computation.8 | convolution fusion | flops 8388608 | bytes 8585216 | tf_op jit(solution)/shard_map/kij,ki->kj/dot_general | solution.py:68
  105.5 0.0 copy-done.4
  105.5 0.2 convolution_convert_fusion.2
  105.7 0.0 copy-done.7
  105.7 0.2 fusion.14
  105.9 0.0 copy-done
  105.9 0.9 fusion.11
  106.8 0.0 copy-done.5
  106.8 0.2 convolution_convert_fusion.1
  107.0 1.9 collective-permute-start
  108.9 3.6 %collective-permute-start.2 = (bf16[64,128]{1,0:T(8,128)(2,1)S(1)}, bf16[64,128]{1,0:T(8,128)(2,1)S(1)}, u32[]{:S(2)}, u32[]{:S(2)}) collective-permute-start(bf16[64,128]{1,0:T(8,128)(2,1)S(1)} %convolution_convert_fusion.1), channel_id=1, source_target_pairs={{16,0},{32,16},{48,32},{64,48},{80,64},{96,80},{112,96},{128,112},... | collective-permute-start | bytes 49160 | tf_op jit(solution)/shard_map/ppermute | solution.py:31
  112.6 0.0 collective-permute-done.1
  112.6 0.0 collective-permute-done
  112.6 1.4 collective-permute-done.2
  114.0 0.2 fusion.13
  114.2 7.8 %fusion.4 = f32[256,1,128]{2,1,0:T(1,128)S(1)} fusion(bf16[1,256,128,128]{3,2,1,0:T(8,128)(2,1)} %param.16, bf16[256,128,1]{1,0,2:T(8,128)(2,1)S(1)} %fusion.13), kind=kOutput, calls=%fused_computation.6 | convolution fusion | flops 8388608 | bytes 8585216 | tf_op jit(solution)/shard_map/kij,kj->ki/dot_general | solution.py:93
  122.0 0.2 broadcast_in_dim.8
  122.2 1.3 collective-permute-start.3
  123.5 4.2 %collective-permute-start.4 = (bf16[256,128]{1,0:T(8,128)(2,1)S(1)}, bf16[256,128]{1,0:T(8,128)(2,1)S(1)}, u32[]{:S(2)}, u32[]{:S(2)}) collective-permute-start(bf16[256,128]{1,0:T(8,128)(2,1)S(1)} %get-tuple-element.6), channel_id=1, source_target_pairs={{0,15},{1,0},{2,1},{3,2},{4,3},{5,4},{6,5},{7,6},{8,7},{9,8},{10,9... | collective-permute-start | bytes 196616 | tf_op jit(solution)/shard_map/ppermute | solution.py:21
  127.6 0.0 copy-done.2
  127.9 0.0 copy-done.1
  127.9 2.0 collective-permute-done.3
  129.9 0.0 collective-permute-start.5
  129.9 0.0 collective-permute-done.4
  129.9 5.6 %collective-permute-start.6 = (bf16[256,128]{1,0:T(8,128)(2,1)S(1)}, bf16[256,128]{1,0:T(8,128)(2,1)S(1)}, u32[]{:S(2)}, u32[]{:S(2)}) collective-permute-start(bf16[256,128]{1,0:T(8,128)(2,1)S(1)} %collective-permute-done.4), channel_id=1, source_target_pairs={{0,15},{1,0},{2,1},{3,2},{4,3},{5,4},{6,5},{7,6},{8,7},{9,8},{10,9... | collective-permute-start | bytes 196616 | tf_op jit(solution)/shard_map/ppermute | solution.py:21
  135.5 2.1 %collective-permute-done.5 = bf16[256,128]{1,0:T(8,128)(2,1)S(1)} collective-permute-done((bf16[256,128]{1,0:T(8,128)(2,1)S(1)}, bf16[256,128]{1,0:T(8,128)(2,1)S(1)}, u32[]{:S(2)}, u32[]{:S(2)}) %collective-permute-start.5) | collective-permute-done | bytes 65568 | tf_op jit(solution)/shard_map/ppermute | solution.py:16
  137.7 0.0 collective-permute-start.7
  137.7 0.0 collective-permute-done.6
  137.7 5.4 %collective-permute-start.8 = (bf16[256,128]{1,0:T(8,128)(2,1)S(1)}, bf16[256,128]{1,0:T(8,128)(2,1)S(1)}, u32[]{:S(2)}, u32[]{:S(2)}) collective-permute-start(bf16[256,128]{1,0:T(8,128)(2,1)S(1)} %collective-permute-done.6), channel_id=1, source_target_pairs={{0,15},{1,0},{2,1},{3,2},{4,3},{5,4},{6,5},{7,6},{8,7},{9,8},{10,9... | collective-permute-start | bytes 196616 | tf_op jit(solution)/shard_map/ppermute | solution.py:21
  143.1 2.1 %collective-permute-done.7 = bf16[256,128]{1,0:T(8,128)(2,1)S(1)} collective-permute-done((bf16[256,128]{1,0:T(8,128)(2,1)S(1)}, bf16[256,128]{1,0:T(8,128)(2,1)S(1)}, u32[]{:S(2)}, u32[]{:S(2)}) %collective-permute-start.7) | collective-permute-done | bytes 65568 | tf_op jit(solution)/shard_map/ppermute | solution.py:16
  145.3 0.0 collective-permute-start.9
  145.3 0.0 collective-permute-done.8
  145.3 5.4 %collective-permute-start.10 = (bf16[256,128]{1,0:T(8,128)(2,1)S(1)}, bf16[256,128]{1,0:T(8,128)(2,1)S(1)}, u32[]{:S(2)}, u32[]{:S(2)}) collective-permute-start(bf16[256,128]{1,0:T(8,128)(2,1)S(1)} %collective-permute-done.8), channel_id=1, source_target_pairs={{0,15},{1,0},{2,1},{3,2},{4,3},{5,4},{6,5},{7,6},{8,7},{9,8},{10,9... | collective-permute-start | bytes 196616 | tf_op jit(solution)/shard_map/ppermute | solution.py:21
  150.7 2.1 %collective-permute-done.9 = bf16[256,128]{1,0:T(8,128)(2,1)S(1)} collective-permute-done((bf16[256,128]{1,0:T(8,128)(2,1)S(1)}, bf16[256,128]{1,0:T(8,128)(2,1)S(1)}, u32[]{:S(2)}, u32[]{:S(2)}) %collective-permute-start.9) | collective-permute-done | bytes 65568 | tf_op jit(solution)/shard_map/ppermute | solution.py:16
  152.9 0.0 collective-permute-start.11
  152.9 0.0 collective-permute-done.10
  152.9 5.4 %collective-permute-start.12 = (bf16[256,128]{1,0:T(8,128)(2,1)S(1)}, bf16[256,128]{1,0:T(8,128)(2,1)S(1)}, u32[]{:S(2)}, u32[]{:S(2)}) collective-permute-start(bf16[256,128]{1,0:T(8,128)(2,1)S(1)} %collective-permute-done.10), channel_id=1, source_target_pairs={{0,15},{1,0},{2,1},{3,2},{4,3},{5,4},{6,5},{7,6},{8,7},{9,8},{10,9... | collective-permute-start | bytes 196616 | tf_op jit(solution)/shard_map/ppermute | solution.py:21
  158.3 2.1 %collective-permute-done.11 = bf16[256,128]{1,0:T(8,128)(2,1)S(1)} collective-permute-done((bf16[256,128]{1,0:T(8,128)(2,1)S(1)}, bf16[256,128]{1,0:T(8,128)(2,1)S(1)}, u32[]{:S(2)}, u32[]{:S(2)}) %collective-permute-start.11) | collective-permute-done | bytes 65568 | tf_op jit(solution)/shard_map/ppermute | solution.py:16
  160.5 0.0 collective-permute-start.13
  160.5 0.0 collective-permute-done.12
  160.5 5.4 %collective-permute-start.14 = (bf16[256,128]{1,0:T(8,128)(2,1)S(1)}, bf16[256,128]{1,0:T(8,128)(2,1)S(1)}, u32[]{:S(2)}, u32[]{:S(2)}) collective-permute-start(bf16[256,128]{1,0:T(8,128)(2,1)S(1)} %collective-permute-done.12), channel_id=1, source_target_pairs={{0,15},{1,0},{2,1},{3,2},{4,3},{5,4},{6,5},{7,6},{8,7},{9,8},{10,9... | collective-permute-start | bytes 196616 | tf_op jit(solution)/shard_map/ppermute | solution.py:21
  165.9 2.1 %collective-permute-done.13 = bf16[256,128]{1,0:T(8,128)(2,1)S(1)} collective-permute-done((bf16[256,128]{1,0:T(8,128)(2,1)S(1)}, bf16[256,128]{1,0:T(8,128)(2,1)S(1)}, u32[]{:S(2)}, u32[]{:S(2)}) %collective-permute-start.13) | collective-permute-done | bytes 65568 | tf_op jit(solution)/shard_map/ppermute | solution.py:16
  168.0 0.0 collective-permute-start.15
  168.0 0.0 collective-permute-done.14
  168.0 5.4 %collective-permute-start.16 = (bf16[256,128]{1,0:T(8,128)(2,1)S(1)}, bf16[256,128]{1,0:T(8,128)(2,1)S(1)}, u32[]{:S(2)}, u32[]{:S(2)}) collective-permute-start(bf16[256,128]{1,0:T(8,128)(2,1)S(1)} %collective-permute-done.14), channel_id=1, source_target_pairs={{0,15},{1,0},{2,1},{3,2},{4,3},{5,4},{6,5},{7,6},{8,7},{9,8},{10,9... | collective-permute-start | bytes 196616 | tf_op jit(solution)/shard_map/ppermute | solution.py:21
  173.5 2.3 %collective-permute-done.15 = bf16[256,128]{1,0:T(8,128)(2,1)S(1)} collective-permute-done((bf16[256,128]{1,0:T(8,128)(2,1)S(1)}, bf16[256,128]{1,0:T(8,128)(2,1)S(1)}, u32[]{:S(2)}, u32[]{:S(2)}) %collective-permute-start.15) | collective-permute-done | bytes 65568 | tf_op jit(solution)/shard_map/ppermute | solution.py:16
  175.8 0.0 collective-permute-start.17
  175.8 0.0 collective-permute-done.16
  175.9 7.5 %collective-permute-done.17 = bf16[256,128]{1,0:T(8,128)(2,1)S(1)} collective-permute-done((bf16[256,128]{1,0:T(8,128)(2,1)S(1)}, bf16[256,128]{1,0:T(8,128)(2,1)S(1)}, u32[]{:S(2)}, u32[]{:S(2)}) %collective-permute-start.17) | collective-permute-done | bytes 65568 | tf_op jit(solution)/shard_map/ppermute | solution.py:16
  183.4 0.0 copy-done.6
  183.4 7.0 %fusion.10 = bf16[1,2048,128]{2,1,0:T(8,128)(2,1)} fusion(bf16[4096,128]{1,0:T(8,128)(2,1)S(1)} %constant_dynamic-update-slice_fusion, s32[2048]{0:T(1024)S(1)} %add.141, s32[2048]{0:T(1024)S(1)} %bitcast.56), kind=kOutput, calls=%fused_computation.12 | convolution fusion | flops 2156658688 | bytes 1589248 | tf_op jit(solution)/shard_map/dot_general | solution.py:99
  (21 shorter events, 0.3 us)
Async XLA Ops:
  6.5 99.4 %copy-start = (bf16[1,48,128,128]{3,2,1,0:T(8,128)(2,1)S(1)}, bf16[1,48,128,128]{3,2,1,0:T(8,128)(2,1)}, u32[]{:S(2)}) copy-start(bf16[1,48,128,128]{3,2,1,0:T(8,128)(2,1)} %param.18) | copy-start | bytes 4718596
  6.5 92.4 %reduce-scatter.2.cloned.1.call-start = ((), (), s32[]{:S(2)}) async-start(), calls=%async_computation.1 | async-start | bytes 2228224 | tf_op jit(solution)/shard_map/reduce_scatter | solution.py:61
  7.4 8.6 %copy-start.3 = (bf16[1,64,128]{2,1,0:T(8,128)(2,1)S(1)}, bf16[1,64,128]{2,1,0:T(8,128)(2,1)}, u32[]{:S(2)}) copy-start(bf16[1,64,128]{2,1,0:T(8,128)(2,1)} %param.21) | copy-start | bytes 49156
  16.0 89.5 %copy-start.4 = (s32[1,256]{1,0:T(1,128)S(1)}, s32[1,256]{1,0:T(1,128)}, u32[]{:S(2)}) copy-start(s32[1,256]{1,0:T(1,128)} %param.17) | copy-start | bytes 3076
  16.0 89.7 %copy-start.7 = (s32[1,48]{1,0:T(1,128)S(1)}, s32[1,48]{1,0:T(1,128)}, u32[]{:S(2)}) copy-start(s32[1,48]{1,0:T(1,128)} %param.20) | copy-start | bytes 580
  16.0 90.8 %copy-start.5 = (s32[1,48]{1,0:T(1,128)S(1)}, s32[1,48]{1,0:T(1,128)}, u32[]{:S(2)}) copy-start(s32[1,48]{1,0:T(1,128)} %param.19) | copy-start | bytes 580
  16.0 96.6 %collective-permute-start.1 = (bf16[64,128]{1,0:T(8,128)(2,1)S(1)}, bf16[64,128]{1,0:T(8,128)(2,1)S(1)}, u32[]{:S(2)}, u32[]{:S(2)}) collective-permute-start(bf16[64,128]{1,0:T(8,128)(2,1)S(1)} %bitcast.50), channel_id=1, source_target_pairs={{16,0},{32,16},{48,32},{64,48},{80,64},{96,80},{112,96},{128,112},... | collective-permute-start | bytes 49160 | tf_op jit(solution)/shard_map/ppermute | solution.py:31
  99.8 27.8 %copy-start.2 = (s32[1,2048,1]{1,2,0:T(1,128)S(1)}, s32[1,2048,1]{1,2,0:T(1,128)}, u32[]{:S(2)}) copy-start(s32[1,2048,1]{1,2,0:T(1,128)} %param.14) | copy-start | bytes 24580
  105.5 22.4 %copy-start.1 = (s32[1,2048]{1,0:T(1,128)S(1)}, s32[1,2048]{1,0:T(1,128)}, u32[]{:S(2)}) copy-start(s32[1,2048]{1,0:T(1,128)} %param.15) | copy-start | bytes 24580
  105.5 77.9 %copy-start.6 = (s32[1,2048]{1,0:T(1,128)S(1)}, s32[1,2048]{1,0:T(1,128)}, u32[]{:S(2)}) copy-start(s32[1,2048]{1,0:T(1,128)} %param.13) | copy-start | bytes 24580
  107.0 5.6 %collective-permute-start = (bf16[64,128]{1,0:T(8,128)(2,1)S(1)}, bf16[64,128]{1,0:T(8,128)(2,1)S(1)}, u32[]{:S(2)}, u32[]{:S(2)}) collective-permute-start(bf16[64,128]{1,0:T(8,128)(2,1)S(1)} %convolution_convert_fusion.1), channel_id=1, source_target_pairs={{0,16},{16,32},{32,48},{48,64},{64,80},{80,96},{96,112},{112,128},... | collective-permute-start | bytes 49160 | tf_op jit(solution)/shard_map/ppermute | solution.py:31
  108.9 5.1 %collective-permute-start.2 = (bf16[64,128]{1,0:T(8,128)(2,1)S(1)}, bf16[64,128]{1,0:T(8,128)(2,1)S(1)}, u32[]{:S(2)}, u32[]{:S(2)}) collective-permute-start(bf16[64,128]{1,0:T(8,128)(2,1)S(1)} %convolution_convert_fusion.1), channel_id=1, source_target_pairs={{16,0},{32,16},{48,32},{64,48},{80,64},{96,80},{112,96},{128,112},... | collective-permute-start | bytes 49160 | tf_op jit(solution)/shard_map/ppermute | solution.py:31
  122.2 7.7 %collective-permute-start.3 = (bf16[256,128]{1,0:T(8,128)(2,1)S(1)}, bf16[256,128]{1,0:T(8,128)(2,1)S(1)}, u32[]{:S(2)}, u32[]{:S(2)}) collective-permute-start(bf16[256,128]{1,0:T(8,128)(2,1)S(1)} %get-tuple-element.6), channel_id=1, source_target_pairs={{0,1},{1,2},{2,3},{3,4},{4,5},{5,6},{6,7},{7,8},{8,9},{9,10},{10,1... | collective-permute-start | bytes 196616 | tf_op jit(solution)/shard_map/ppermute | solution.py:16
  123.5 6.4 %collective-permute-start.4 = (bf16[256,128]{1,0:T(8,128)(2,1)S(1)}, bf16[256,128]{1,0:T(8,128)(2,1)S(1)}, u32[]{:S(2)}, u32[]{:S(2)}) collective-permute-start(bf16[256,128]{1,0:T(8,128)(2,1)S(1)} %get-tuple-element.6), channel_id=1, source_target_pairs={{0,15},{1,0},{2,1},{3,2},{4,3},{5,4},{6,5},{7,6},{8,7},{9,8},{10,9... | collective-permute-start | bytes 196616 | tf_op jit(solution)/shard_map/ppermute | solution.py:21
  129.9 7.8 %collective-permute-start.5 = (bf16[256,128]{1,0:T(8,128)(2,1)S(1)}, bf16[256,128]{1,0:T(8,128)(2,1)S(1)}, u32[]{:S(2)}, u32[]{:S(2)}) collective-permute-start(bf16[256,128]{1,0:T(8,128)(2,1)S(1)} %collective-permute-done.3), channel_id=1, source_target_pairs={{0,1},{1,2},{2,3},{3,4},{4,5},{5,6},{6,7},{7,8},{8,9},{9,10},{10,1... | collective-permute-start | bytes 196616 | tf_op jit(solution)/shard_map/ppermute | solution.py:16
  129.9 7.8 %collective-permute-start.6 = (bf16[256,128]{1,0:T(8,128)(2,1)S(1)}, bf16[256,128]{1,0:T(8,128)(2,1)S(1)}, u32[]{:S(2)}, u32[]{:S(2)}) collective-permute-start(bf16[256,128]{1,0:T(8,128)(2,1)S(1)} %collective-permute-done.4), channel_id=1, source_target_pairs={{0,15},{1,0},{2,1},{3,2},{4,3},{5,4},{6,5},{7,6},{8,7},{9,8},{10,9... | collective-permute-start | bytes 196616 | tf_op jit(solution)/shard_map/ppermute | solution.py:21
  137.7 7.6 %collective-permute-start.7 = (bf16[256,128]{1,0:T(8,128)(2,1)S(1)}, bf16[256,128]{1,0:T(8,128)(2,1)S(1)}, u32[]{:S(2)}, u32[]{:S(2)}) collective-permute-start(bf16[256,128]{1,0:T(8,128)(2,1)S(1)} %collective-permute-done.5), channel_id=1, source_target_pairs={{0,1},{1,2},{2,3},{3,4},{4,5},{5,6},{6,7},{7,8},{8,9},{9,10},{10,1... | collective-permute-start | bytes 196616 | tf_op jit(solution)/shard_map/ppermute | solution.py:16
  137.7 7.6 %collective-permute-start.8 = (bf16[256,128]{1,0:T(8,128)(2,1)S(1)}, bf16[256,128]{1,0:T(8,128)(2,1)S(1)}, u32[]{:S(2)}, u32[]{:S(2)}) collective-permute-start(bf16[256,128]{1,0:T(8,128)(2,1)S(1)} %collective-permute-done.6), channel_id=1, source_target_pairs={{0,15},{1,0},{2,1},{3,2},{4,3},{5,4},{6,5},{7,6},{8,7},{9,8},{10,9... | collective-permute-start | bytes 196616 | tf_op jit(solution)/shard_map/ppermute | solution.py:21
  145.3 7.6 %collective-permute-start.9 = (bf16[256,128]{1,0:T(8,128)(2,1)S(1)}, bf16[256,128]{1,0:T(8,128)(2,1)S(1)}, u32[]{:S(2)}, u32[]{:S(2)}) collective-permute-start(bf16[256,128]{1,0:T(8,128)(2,1)S(1)} %collective-permute-done.7), channel_id=1, source_target_pairs={{0,1},{1,2},{2,3},{3,4},{4,5},{5,6},{6,7},{7,8},{8,9},{9,10},{10,1... | collective-permute-start | bytes 196616 | tf_op jit(solution)/shard_map/ppermute | solution.py:16
  145.3 7.6 %collective-permute-start.10 = (bf16[256,128]{1,0:T(8,128)(2,1)S(1)}, bf16[256,128]{1,0:T(8,128)(2,1)S(1)}, u32[]{:S(2)}, u32[]{:S(2)}) collective-permute-start(bf16[256,128]{1,0:T(8,128)(2,1)S(1)} %collective-permute-done.8), channel_id=1, source_target_pairs={{0,15},{1,0},{2,1},{3,2},{4,3},{5,4},{6,5},{7,6},{8,7},{9,8},{10,9... | collective-permute-start | bytes 196616 | tf_op jit(solution)/shard_map/ppermute | solution.py:21
  152.9 7.6 %collective-permute-start.11 = (bf16[256,128]{1,0:T(8,128)(2,1)S(1)}, bf16[256,128]{1,0:T(8,128)(2,1)S(1)}, u32[]{:S(2)}, u32[]{:S(2)}) collective-permute-start(bf16[256,128]{1,0:T(8,128)(2,1)S(1)} %collective-permute-done.9), channel_id=1, source_target_pairs={{0,1},{1,2},{2,3},{3,4},{4,5},{5,6},{6,7},{7,8},{8,9},{9,10},{10,1... | collective-permute-start | bytes 196616 | tf_op jit(solution)/shard_map/ppermute | solution.py:16
  152.9 7.6 %collective-permute-start.12 = (bf16[256,128]{1,0:T(8,128)(2,1)S(1)}, bf16[256,128]{1,0:T(8,128)(2,1)S(1)}, u32[]{:S(2)}, u32[]{:S(2)}) collective-permute-start(bf16[256,128]{1,0:T(8,128)(2,1)S(1)} %collective-permute-done.10), channel_id=1, source_target_pairs={{0,15},{1,0},{2,1},{3,2},{4,3},{5,4},{6,5},{7,6},{8,7},{9,8},{10,9... | collective-permute-start | bytes 196616 | tf_op jit(solution)/shard_map/ppermute | solution.py:21
  160.5 7.6 %collective-permute-start.13 = (bf16[256,128]{1,0:T(8,128)(2,1)S(1)}, bf16[256,128]{1,0:T(8,128)(2,1)S(1)}, u32[]{:S(2)}, u32[]{:S(2)}) collective-permute-start(bf16[256,128]{1,0:T(8,128)(2,1)S(1)} %collective-permute-done.11), channel_id=1, source_target_pairs={{0,1},{1,2},{2,3},{3,4},{4,5},{5,6},{6,7},{7,8},{8,9},{9,10},{10,1... | collective-permute-start | bytes 196616 | tf_op jit(solution)/shard_map/ppermute | solution.py:16
  160.5 7.6 %collective-permute-start.14 = (bf16[256,128]{1,0:T(8,128)(2,1)S(1)}, bf16[256,128]{1,0:T(8,128)(2,1)S(1)}, u32[]{:S(2)}, u32[]{:S(2)}) collective-permute-start(bf16[256,128]{1,0:T(8,128)(2,1)S(1)} %collective-permute-done.12), channel_id=1, source_target_pairs={{0,15},{1,0},{2,1},{3,2},{4,3},{5,4},{6,5},{7,6},{8,7},{9,8},{10,9... | collective-permute-start | bytes 196616 | tf_op jit(solution)/shard_map/ppermute | solution.py:21
  168.0 7.8 %collective-permute-start.15 = (bf16[256,128]{1,0:T(8,128)(2,1)S(1)}, bf16[256,128]{1,0:T(8,128)(2,1)S(1)}, u32[]{:S(2)}, u32[]{:S(2)}) collective-permute-start(bf16[256,128]{1,0:T(8,128)(2,1)S(1)} %collective-permute-done.13), channel_id=1, source_target_pairs={{0,1},{1,2},{2,3},{3,4},{4,5},{5,6},{6,7},{7,8},{8,9},{9,10},{10,1... | collective-permute-start | bytes 196616 | tf_op jit(solution)/shard_map/ppermute | solution.py:16
  168.0 7.8 %collective-permute-start.16 = (bf16[256,128]{1,0:T(8,128)(2,1)S(1)}, bf16[256,128]{1,0:T(8,128)(2,1)S(1)}, u32[]{:S(2)}, u32[]{:S(2)}) collective-permute-start(bf16[256,128]{1,0:T(8,128)(2,1)S(1)} %collective-permute-done.14), channel_id=1, source_target_pairs={{0,15},{1,0},{2,1},{3,2},{4,3},{5,4},{6,5},{7,6},{8,7},{9,8},{10,9... | collective-permute-start | bytes 196616 | tf_op jit(solution)/shard_map/ppermute | solution.py:21
  175.8 7.6 %collective-permute-start.17 = (bf16[256,128]{1,0:T(8,128)(2,1)S(1)}, bf16[256,128]{1,0:T(8,128)(2,1)S(1)}, u32[]{:S(2)}, u32[]{:S(2)}) collective-permute-start(bf16[256,128]{1,0:T(8,128)(2,1)S(1)} %collective-permute-done.15), channel_id=1, source_target_pairs={{0,1},{1,2},{2,3},{3,4},{4,5},{5,6},{6,7},{7,8},{8,9},{9,10},{10,1... | collective-permute-start | bytes 196616 | tf_op jit(solution)/shard_map/ppermute | solution.py:16
Sparse Core Ops, SparseCore 0:
  16.1 82.7 reduce-scatter.1
